TPU v7x, 128 devices: a whole 4x4x4 slice. The times are simulated.
128 devices in a mesh: tok: 16 (over x, z), row: 4 (over y), col: 2 (over core).
Axes of the slice: x: 4, y: 4, z: 4, core: 2. Of those that a mesh axis runs over, the one named last changes fastest.
Arguments:
- block_input_rows: bfloat16 [8192, 4096], P(('tok', 'row'), 'col'), may hold values from -18 to 18
- input_norm_scale: bfloat16 [4096], P('col'), may hold values from 0.6 to 10, as said below
- query_key_value_weight: bfloat16 [4096, 16, 3, 128], P('col', 'row'), may hold values from -0.09375 to 0.09375
- adapter_down_weight: bfloat16 [4096, 128], P('col'), may hold values from -0.09375 to 0.09375
- adapter_up_weight: bfloat16 [128, 16, 3, 128], P(None, 'row'), may hold values from -0.5 to 0.5
- output_projection_weight: bfloat16 [2048, 2048], P(('row', 'col')), may hold values from -0.125 to 0.125
- prompt_segment_index: int32 [8192], replicated, may hold values from 0 to 3, never falling along the last dimension, each value on 1 to 4352 neighbouring positions
- cache_owner_index: int32 [8192, 1], P('tok'), may hold values from 0 to 15; in each aligned block of 512 rows (0 to 511, 512 to 1023, ...) at most 64 rows name the same one
Outputs:
- block_output: bfloat16 [8192, 2048], P(('tok', 'row', 'col'))
- kv_cache: bfloat16 [16384, 16, 2, 128], P('tok', ('row', 'col'))
Inputs may be any that keep to these rules, and one draw needn't show every extreme that they name: `prompt_segment_index`: never falls along the tokens; every prompt holds 1 to 4352 tokens and one holds exactly 4352. `cache_owner_index`: in each aligned block of 512 tokens no owner is named by more than 64 tokens; some owner is named exactly 64 times in some block. `input_norm_scale`: positive gains.
All inputs are finite; a program needn't handle non-finite values.
Results may differ from a plain program's by a relative error of at most 0.015.
The roundings to bfloat16 on the way count: a program that leaves them out, or rounds other values in their place, can miss the bound.
Values may be sent and summed in bfloat16 or wider, within the bound.
No kernel may reach another device: no remote copies, remote signals or barrier semaphores. Data moves between devices by JAX's collectives and lax.ppermute only.
A program may use at most 192 MiB of HBM per device.

v0:
```python
import jax
import jax.numpy as jnp
from jax import lax
from jax.sharding import PartitionSpec as P

INPUT_WIDTH = 4096
HEAD_SIZE = 128
ADAPTER_RANK = 128


def fold_piece(carry, piece, query, own_seg, own_start, prompt_segment_index, scale):
    top_old, total_old, acc_old = carry
    count = piece.shape[0]
    key_pos = jnp.arange(count, dtype=jnp.int32)
    query_pos = own_start + jnp.arange(query.shape[1], dtype=jnp.int32)
    allowed = (
        (own_seg[:, None] == prompt_segment_index[None, :])
        & (key_pos[None, :] <= query_pos[:, None])
        & (key_pos[None, :] >= 0)
    )
    score = (
        jnp.einsum("htd,shd->hts", query, piece[:, :, 0], preferred_element_type=jnp.float32)
        * scale
    )
    masked = jnp.where(allowed[None], score, -1e30)
    top_new = jnp.maximum(top_old, jnp.max(masked, axis=2))
    weights = jnp.where(allowed[None], jnp.exp(score - top_new[:, :, None]), 0.0).astype(
        jnp.bfloat16
    )
    total_new = jnp.sum(weights.astype(jnp.float32), axis=2)
    acc_new = jnp.einsum(
        "hts,shd->htd", weights, piece[:, :, 1], preferred_element_type=jnp.float32
    )
    return (top_new, total_new, acc_new)


def shards(
    block_input_rows,
    input_norm_scale,
    query_key_value_weight,
    adapter_down_weight,
    adapter_up_weight,
    output_projection_weight,
    prompt_segment_index,
    cache_owner_index,
):
    gathered = lax.all_gather(block_input_rows, "row", axis=0, tiled=True)
    wide = gathered.astype(jnp.float32)
    partial_sq = jnp.sum(wide * wide, axis=1)
    total_sq = lax.psum(partial_sq, "col")
    inverse = lax.rsqrt(total_sq / INPUT_WIDTH + 1e-06)
    normalized_input = (
        wide * inverse[:, None] * input_norm_scale.astype(jnp.float32)[None, :]
    ).astype(jnp.bfloat16)
    adapter_hidden = jnp.dot(
        normalized_input, adapter_down_weight, preferred_element_type=jnp.float32
    )
    tok_dev = gathered.shape[0]
    local_head_count = query_key_value_weight.shape[1]
    flat_weight = query_key_value_weight.reshape(
        query_key_value_weight.shape[0], local_head_count, 3 * HEAD_SIZE
    )
    flattened_up_weight = adapter_up_weight.reshape(ADAPTER_RANK, local_head_count, 3 * HEAD_SIZE)
    heads_dev = local_head_count // lax.axis_size("col")
    main = jnp.einsum(
        "td,dhe->hte", normalized_input, flat_weight, preferred_element_type=jnp.float32
    )
    adapter_down_output = jnp.einsum(
        "tr,rhe->hte",
        adapter_hidden,
        flattened_up_weight.astype(jnp.float32),
        precision=lax.Precision.HIGHEST,
    )
    mixed = lax.psum_scatter(main + adapter_down_output, "col", scatter_dimension=0, tiled=True)
    qkv = mixed.astype(jnp.bfloat16).reshape(heads_dev, tok_dev, 3, HEAD_SIZE)
    query = qkv[:, :, 0]
    kv_tok = jnp.transpose(qkv[:, :, 1:3], (1, 0, 2, 3))
    own_start = lax.axis_index("tok") * tok_dev
    own_seg = lax.dynamic_slice_in_dim(prompt_segment_index, own_start, tok_dev, 0)
    scale = 1.0 / HEAD_SIZE**0.5
    init = (
        jnp.full((heads_dev, tok_dev), -1e30, jnp.float32),
        jnp.zeros((heads_dev, tok_dev), jnp.float32),
        jnp.zeros((heads_dev, tok_dev, HEAD_SIZE), jnp.float32),
    )
    state = fold_piece(
        init,
        lax.all_gather(kv_tok, "tok", axis=0, tiled=True),
        query,
        own_seg,
        own_start,
        prompt_segment_index,
        scale,
    )
    attended = (state[2] / state[1][:, :, None]).astype(jnp.bfloat16)
    attended = jnp.transpose(attended, (1, 0, 2)).reshape(tok_dev, heads_dev * HEAD_SIZE)
    block_output = lax.psum_scatter(
        jnp.dot(attended, output_projection_weight, preferred_element_type=jnp.float32).astype(
            jnp.bfloat16
        ),
        ("row", "col"),
        scatter_dimension=0,
        tiled=True,
    )
    count_tok = lax.axis_size("tok")
    capacity = max(2, 2 * tok_dev // count_tok)
    owner = cache_owner_index[:, 0]
    onehot = (owner[:, None] == jnp.arange(count_tok, dtype=jnp.int32)[None, :]).astype(jnp.int32)
    before = jnp.cumsum(onehot, axis=0) - onehot
    rank = jnp.sum(before * onehot, axis=1)
    slot = owner * capacity + rank
    selector = (jnp.arange(count_tok * capacity, dtype=jnp.int32)[:, None] == slot[None, :]).astype(
        jnp.bfloat16
    )
    outgoing = jnp.dot(
        selector,
        kv_tok.reshape(tok_dev, heads_dev * 2 * HEAD_SIZE),
        preferred_element_type=jnp.float32,
    ).astype(jnp.bfloat16)
    received = lax.all_to_all(outgoing, "tok", split_axis=0, concat_axis=0, tiled=True)
    kv_cache = received.reshape(count_tok * capacity, heads_dev, 2, HEAD_SIZE)
    return (block_output, kv_cache)


def solution(mesh):
    placed = (
        P(("tok", "row"), "col"),
        P("col"),
        P("col", "row", None, None),
        P("col", None),
        P(None, "row", None, None),
        P(("row", "col"), None),
        P(),
        P("tok", None),
    )
    return jax.shard_map(
        shards,
        mesh=mesh,
        in_specs=placed,
        out_specs=(P(("tok", "row", "col"), None), P("tok", ("row", "col"), None, None)),
        check_vma=False,
    )
```

profile of v0, /device:TPU:0, one launch (start us, length us, event | category | flops | bytes accessed | tf_op | source)
XLA Modules:
  0.0 240.3 jit_solution(15088219014091748765)
XLA Ops:
  7.2 0.0 all-gather.3.cloned.1.call-start
  7.2 0.7 all-gather.3.cloned.1.call-update
  7.9 0.0 reduce-scatter.3.cloned.1.call-start
  8.0 0.7 convert_element_type.38
  8.7 10.7 %copy.13 = bf16[2048,4,3,128]{0,3,2,1:T(8,128)(2,1)} copy(bf16[2048,4,3,128]{3,1,2,0:T(4,128)(2,1)} %param.10) | data formatting | bytes 12582912 | tf_op args[2]
  19.4 0.3 copy.15
  19.7 23.3 %all-gather.3.cloned.1.call-done = bf16[512,2048]{1,0:T(8,128)(2,1)} async-done(((bf16[128,2048]{1,0:T(8,128)(2,1)}), bf16[512,2048]{1,0:T(8,128)(2,1)}) %all-gather.3.cloned.1.call-update) | async-done | bytes 2097168 | tf_op jit(solution)/shard_map/all_gather | solution.py:47
  43.0 2.1 fusion.1
  45.0 2.5 %psum.7 = f32[512]{0:T(512)S(1)} all-reduce(f32[512]{0:T(512)S(1)} %fusion.1), channel_id=1, replica_groups=mesh['tok'=16,'row'=4,'col'=2] {'col'}, use_global_device_ids=true, to_apply=%region_1.0 | all-reduce | flops 512 | bytes 4096 | tf_op jit(solution)/shard_map/psum | solution.py:50
  47.5 6.4 %fusion.6 = f32[512,4,384]{2,0,1:T(8,128)S(1)} fusion(bf16[2048,4,384]{0,2,1:T(8,128)(2,1)} %bitcast.71, bf16[512,2048]{1,0:T(8,128)(2,1)} %all-gather.3.cloned.1.call-done, f32[2048]{0:T(1024)S(1)} %convert_element_type.38, f32[512]{0:T(512)S(1)} %add_rsqrt_fusion), kind=kOutput, calls=%fused_computation.16 | convolution fusion | flops 3225419776 | bytes 11544576 | tf_op jit(solution)/shard_map/td,dhe->hte/dot_general | solution.py:65
  53.9 0.8 convolution_bitcast_fusion
  54.7 3.2 %add_bitcast_fusion = f32[4,512,384]{2,1,0:T(8,128)} fusion(f32[512,4,384]{2,0,1:T(8,128)S(1)} %fusion.6, f32[512,128,1]{1,0,2:T(8,128)S(1)} %convolution_bitcast_fusion, bf16[128,4,384]{0,2,1:T(8,128)(2,1)S(1)} %bitcast.76), kind=kOutput, calls=%fused_computation.14 | convolution fusion | flops 1208745984 | bytes 6946816 | tf_op jit(solution)/shard_map/tr,rhe->hte/dot_general | solution.py:68
  57.9 0.0 all-gather.5.cloned.1.call-start
  58.0 14.1 %reduce-scatter.3.cloned.1.call-done = f32[2,512,384]{2,1,0:T(8,128)} async-done(((f32[4,512,384]{2,1,0:T(8,128)}), f32[2,512,384]{2,1,0:T(8,128)}) %reduce-scatter.3.cloned.1.call-update) | async-done | bytes 1572880 | tf_op jit(solution)/shard_map/reduce_scatter | solution.py:74
  72.0 1.5 convert_element_type.40
  73.5 0.3 copy.17
  73.9 1.0 copy.27
  74.9 0.2 reduce-scatter.5.cloned.1.call-start
  75.1 0.1 dynamic_slice.3
  75.2 4.8 %fusion = pred[512,8192]{1,0:T(8,128)(4,1)} fusion(s32[512]{0:T(512)S(1)} %iota_add_fusion, s32[8192]{0:T(1024)S(1)} %copy-done.4, s32[512]{0:T(512)S(1)} %dynamic_slice.3), kind=kLoop, calls=%fused_computation.4 | loop fusion | flops 12582912 | bytes 4231168 | tf_op jit(solution)/shard_map/and | solution.py:17
  80.1 67.3 %all-gather.5.cloned.1.call-done = bf16[8192,2,2,128]{3,0,1,2:T(8,128)(2,1)} async-done(((bf16[512,2,2,128]{3,0,1,2:T(8,128)(2,1)}), bf16[8192,2,2,128]{3,0,1,2:T(8,128)(2,1)}) %all-gather.5.cloned.1.call-update) | async-done | bytes 8388624 | tf_op jit(solution)/shard_map/all_gather | solution.py:88
  147.4 17.6 %select_reduce_fusion = (f32[2,512]{1,0:T(2,128)S(1)}, f32[2,512,8192]{2,1,0:T(8,128)}) fusion(pred[512,8192]{1,0:T(8,128)(4,1)} %fusion, bf16[8192,2,2,128]{3,0,1,2:T(8,128)(2,1)} %all-gather.5.cloned.1.call-done, bf16[2,512,3,128]{1,3,2,0:T(8,128)(2,1)S(1)} %bitcast.73), kind=kOutput, calls=%fused_computation.2 | convolution fusion | flops 2172648448 | bytes 42209280 | tf_op jit(solution)/shard_map/htd,shd->hts/dot_general | solution.py:22
  164.9 16.2 %convert_reduce_fusion = f32[2,512]{1,0:T(2,128)S(1)} fusion(f32[2,512]{1,0:T(2,128)S(1)} %broadcast_maximum_fusion, f32[2,512,8192]{2,1,0:T(8,128)} %get-tuple-element.3, pred[512,8192]{1,0:T(8,128)(4,1)} %fusion), kind=kLoop, calls=%fused_computation | loop fusion | flops 50330624 | bytes 37756928 | tf_op jit(solution)/shard_map/reduce_sum | solution.py:30
  181.1 16.5 %fusion.12 = bf16[512,2,128]{0,2,1:T(8,128)(2,1)S(1)} fusion(bf16[8192,2,2,128]{3,0,1,2:T(8,128)(2,1)} %all-gather.5.cloned.1.call-done, f32[512,2]{0,1:T(2,128)S(1)} %bitcast.82, f32[2,512,8192]{2,1,0:T(8,128)} %get-tuple-element.3, f32[2,512]{1,0:T(2,128)S(1)} %broadcast_maximum_fusion, pred[512,8192]{1,0:T(8,128)(4,1)S(1)} %copy-done.1), kind=kOutput, calls=%fused_computation.23 | convolution fusion | flops 2181300224 | bytes 42213376 | tf_op jit(solution)/shard_map/hts,shd->htd/dot_general | solution.py:31
  197.7 2.1 convolution_convert_fusion
  199.8 1.2 reduce-window.6
  201.0 0.2 slice_reduce_fusion
  201.2 0.1 fusion.18
  201.3 0.7 fusion.9
  202.1 22.0 %all_to_all.9 = bf16[16,64,512]{2,1,0:T(8,128)(2,1)S(1)} all-to-all(bf16[16,64,512]{2,1,0:T(8,128)(2,1)S(1)} %bitcast.77), channel_id=1, replica_groups=mesh['tok'=16,'row'=4,'col'=2] {'tok'}, dimensions={0} | all-to-all | bytes 2097152 | tf_op jit(solution)/shard_map/all_to_all | solution.py:120
  224.1 1.1 reshape.115
  225.2 8.6 %reduce-scatter.5.cloned.1.call-done = bf16[64,2048]{1,0:T(8,128)(2,1)} async-done(((bf16[512,2048]{1,0:T(8,128)(2,1)}), bf16[64,2048]{1,0:T(8,128)(2,1)}) %reduce-scatter.5.cloned.1.call-update) | async-done | bytes 262160 | tf_op jit(solution)/shard_map/reduce_scatter | solution.py:97
  (25 shorter events, 0.2 us)
Async XLA Ops:
  7.2 190.5 %copy-start = (bf16[256,2048]{1,0:T(8,128)(2,1)S(1)}, bf16[256,2048]{1,0:T(8,128)(2,1)}, u32[]{:S(2)}) copy-start(bf16[256,2048]{1,0:T(8,128)(2,1)} %param.13) | copy-start | bytes 3145732
  7.2 35.8 %all-gather.3.cloned.1.call-start = ((), (), s32[]{:S(2)}) async-start(), calls=%async_computation.3 | async-start | bytes 2621440 | tf_op jit(solution)/shard_map/all_gather | solution.py:47
  7.9 64.1 %reduce-scatter.3.cloned.1.call-start = ((), (), s32[]{:S(2)}) async-start(), calls=%async_computation.4 | async-start | bytes 4718592 | tf_op jit(solution)/shard_map/reduce_scatter | solution.py:74
  8.7 10.7 %copy-start.3 = (bf16[128,4,3,128]{3,1,2,0:T(4,128)(2,1)S(1)}, bf16[128,4,3,128]{3,1,2,0:T(4,128)(2,1)}, u32[]{:S(2)}) copy-start(bf16[128,4,3,128]{3,1,2,0:T(4,128)(2,1)} %param.12) | copy-start | bytes 1179652
  47.5 6.4 %copy-start.2 = (bf16[512,2048]{1,0:T(8,128)(2,1)S(1)}, bf16[512,2048]{1,0:T(8,128)(2,1)}, u32[]{:S(2)}) copy-start(bf16[512,2048]{1,0:T(8,128)(2,1)} %all-gather.3.cloned.1.call-done) | copy-start | bytes 6291460
  47.5 6.4 %copy-start.6 = (bf16[2048,128]{1,0:T(8,128)(2,1)S(1)}, bf16[2048,128]{1,0:T(8,128)(2,1)}, u32[]{:S(2)}) copy-start(bf16[2048,128]{1,0:T(8,128)(2,1)} %param.11) | copy-start | bytes 1572868
  57.9 17.2 %copy-start.4 = (s32[8192]{0:T(1024)S(1)}, s32[8192]{0:T(1024)}, u32[]{:S(2)}) copy-start(s32[8192]{0:T(1024)} %param.14) | copy-start | bytes 98308
  57.9 89.4 %all-gather.5.cloned.1.call-start = ((), (), s32[]{:S(2)}) async-start(), calls=%async_computation.5 | async-start | bytes 8912896 | tf_op jit(solution)/shard_map/all_gather | solution.py:88
  74.9 158.9 %reduce-scatter.5.cloned.1.call-start = ((), (), s32[]{:S(2)}) async-start(), calls=%async_computation.6 | async-start | bytes 2359296 | tf_op jit(solution)/shard_map/reduce_scatter | solution.py:97
  164.9 16.2 %copy-start.1 = (pred[512,8192]{1,0:T(8,128)(4,1)S(1)}, pred[512,8192]{1,0:T(8,128)(4,1)}, u32[]{:S(2)}) copy-start(pred[512,8192]{1,0:T(8,128)(4,1)} %fusion) | copy-start | bytes 12582916
  197.6 2.1 copy-start.5
Sparse Core Ops, SparseCore 0:
  9.6 33.2 all-gather.2
  58.0 13.9 reduce-scatter.2
  75.0 72.3 all-gather.4
  199.9 33.8 reduce-scatter.4
where the time goes:
time: 241 us; the launch traced here: 240 us
  waiting for transfers between devices  114 us (47%)
  matrix products  47.2 us (20%)
  other arithmetic  26.6 us (11%)
  blocking collectives  24.5 us (10%)
  between operations  13.9 us (6%)
  local copies, waits for them, and re-layouts  13.8 us (6%)
    all_gather x1, waiting for transfers between devices, shards(): lax.all_gather(kv_tok, 'tok', axis=0, tiled=True)  67.3 us
    all_gather x1, waiting for transfers between devices, shards(): gathered = lax.all_gather(block_input_rows, 'row', axis=0, tiled=True)  23.3 us
    all_to_all x1, blocking collectives, shards(): lax.all_to_all(outgoing, 'tok', split_axis=0, concat_axis=0, tiled=True)  22 us
    dot_general x1, matrix products, fold_piece(): jnp.einsum('htd,shd->hts', query, piece[:, :, 0], preferred_element_type=...  17.6 us
    dot_general x1, matrix products, fold_piece(): jnp.einsum('hts,shd->htd', weights, piece[:, :, 1], preferred_element_typ...  16.5 us
    reduce_sum x1, other arithmetic, fold_piece(): total_new = jnp.sum(weights.astype(jnp.float32), axis=2)  16.2 us
    reduce_scatter x1, waiting for transfers between devices, shards(): lax.psum_scatter(main + adapter_down_output, 'col', scatter_dimension=0,...  14.1 us
    unnamed x17, local copies, waits for them, and re-layouts  12.1 us
  transfers between devices with their start and end apart: 4, of which 4 were waited for; matrix products, arithmetic and copies ran while one was open for 8% of the time, Pallas kernels for 0%

commit v1 on v0

--- a/solution.py
+++ b/solution.py
@@ -6,6 +6,36 @@
 INPUT_WIDTH = 4096
 HEAD_SIZE = 128
 ADAPTER_RANK = 128
+
+
+def _lead_steps_all(xs, k_dim, original):
+    tall = xs.shape
+    built = xs.reshape(*tall[:k_dim], original, tall[k_dim] // original, *tall[k_dim + 1 :])
+    aux = jnp.moveaxis(built, k_dim, 0)
+    return aux
+
+
+def supply_all_target(mine_x, out_dim):
+    mine_x = jnp.moveaxis(mine_x, 0, out_dim)
+    h_now = mine_x.shape
+    left_arr = mine_x.reshape(
+        *h_now[:out_dim], h_now[out_dim] * h_now[out_dim + 1], *h_now[out_dim + 2 :]
+    )
+    return left_arr
+
+
+def form_members_all_on(arr_in, row_axis, patch, field_in):
+    ready, met_up = (lax.axis_size(row_axis), lax.axis_index(row_axis))
+    piece_now = _lead_steps_all(arr_in, patch, ready)
+    k0 = 1
+    by_rank = [piece_now[met_up]]
+    while k0 < ready:
+        carry_out = piece_now[met_up ^ k0]
+        by_rank.append(lax.ppermute(carry_out, row_axis, [(b, b ^ k0) for b in range(ready)]))
+        k0 += 1
+    piece_now = jnp.stack(by_rank, axis=0)[met_up ^ jnp.arange(ready)]
+    local_next = supply_all_target(piece_now, field_in)
+    return local_next
 
 
 def fold_piece(carry, piece, query, own_seg, own_start, prompt_segment_index, scale):
@@ -117,7 +147,7 @@
         kv_tok.reshape(tok_dev, heads_dev * 2 * HEAD_SIZE),
         preferred_element_type=jnp.float32,
     ).astype(jnp.bfloat16)
-    received = lax.all_to_all(outgoing, "tok", split_axis=0, concat_axis=0, tiled=True)
+    received = form_members_all_on(outgoing, "tok", 0, 0)
     kv_cache = received.reshape(count_tok * capacity, heads_dev, 2, HEAD_SIZE)
     return (block_output, kv_cache)
 

time: 241 us -> 247 us (1.025)
  starting transfers between devices: 0.34 us -> 32.4 us
  blocking collectives: 24.5 us -> 2.47 us
  waiting for transfers between devices: 114 us -> 110 us
    ppermute x0 -> x15, starting transfers between devices: none -> 32.1 us  [form_members_all_on(): lax.ppermute(carry_out, row_axis, [(b, b ^ k0) for b in range(ready)])]
    all_to_all x1 -> x0, blocking collectives: 22 us -> none  [shards(): lax.all_to_all(outgoing, 'tok', split_axis=0, concat_axis=0, tiled=True)]
    reduce_scatter x1, waiting for transfers between devices: 8.58 us -> 0.01 us  [shards(): lax.psum_scatter(jnp.dot(attended, output_projection_weight, preferred_el...]
    ppermute x0 -> x15, waiting for transfers between devices: none -> 5.17 us  [form_members_all_on(): lax.ppermute(carry_out, row_axis, [(b, b ^ k0) for b in range(ready)])]
    unnamed x17 -> x33, local copies, waits for them, and re-layouts: 12.1 us -> 12.1 us
  transfers between devices with their start and end apart: 4 -> 19, of which waited for: 4 -> 5; matrix products, arithmetic and copies ran while one was open for 8% -> 8% of each run, Pallas kernels for 0% -> 0%
where the time goes in v1:
time: 247 us
  waiting for transfers between devices  110 us (45%)
  matrix products  47.4 us (19%)
  starting transfers between devices  32.4 us (13%)
  other arithmetic  26 us (11%)
  local copies, waits for them, and re-layouts  14.6 us (6%)
  between operations  14.2 us (6%)
  blocking collectives  2.47 us (1%)
    all_gather x1, waiting for transfers between devices, shards(): lax.all_gather(kv_tok, 'tok', axis=0, tiled=True)  65.8 us
    ppermute x15, starting transfers between devices, form_members_all_on(): lax.ppermute(carry_out, row_axis, [(b, b ^ k0) for b in range(ready)])  32.1 us
    all_gather x1, waiting for transfers between devices, shards(): gathered = lax.all_gather(block_input_rows, 'row', axis=0, tiled=True)  24 us
    dot_general x1, matrix products, fold_piece(): jnp.einsum('htd,shd->hts', query, piece[:, :, 0], preferred_element_type=...  17.6 us
    dot_general x1, matrix products, fold_piece(): jnp.einsum('hts,shd->htd', weights, piece[:, :, 1], preferred_element_typ...  16.7 us
    reduce_sum x1, other arithmetic, fold_piece(): total_new = jnp.sum(weights.astype(jnp.float32), axis=2)  16.2 us
    reduce_scatter x1, waiting for transfers between devices, shards(): lax.psum_scatter(main + adapter_down_output, 'col', scatter_dimension=0,...  14.1 us
    unnamed x33, local copies, waits for them, and re-layouts  12.1 us
  transfers between devices with their start and end apart: 19, of which 5 were waited for; matrix products, arithmetic and copies ran while one was open for 8% of the time, Pallas kernels for 0%

profile of v1, /device:TPU:0, one launch (start us, length us, event | category | flops | bytes accessed | tf_op | source)
XLA Modules:
  0.0 246.7 jit_solution(2513038588804557553)
XLA Ops:
  8.0 10.7 %copy.13 = bf16[2048,4,3,128]{0,3,2,1:T(8,128)(2,1)} copy(bf16[2048,4,3,128]{3,1,2,0:T(4,128)(2,1)} %param.10) | data formatting | bytes 12582912 | tf_op args[2]
  19.0 24.0 %all-gather.3.cloned.1.call-done = bf16[512,2048]{1,0:T(8,128)(2,1)} async-done(((bf16[128,2048]{1,0:T(8,128)(2,1)}), bf16[512,2048]{1,0:T(8,128)(2,1)}) %all-gather.3.cloned.1.call-update) | async-done | bytes 2097168 | tf_op jit(solution)/shard_map/all_gather | solution.py:77
  43.0 2.1 fusion.1
  45.0 2.5 psum.7
  47.5 6.4 %fusion.6 = f32[512,4,384]{2,0,1:T(8,128)S(1)} fusion(bf16[2048,4,384]{0,2,1:T(8,128)(2,1)} %bitcast.133, bf16[512,2048]{1,0:T(8,128)(2,1)} %all-gather.3.cloned.1.call-done, f32[2048]{0:T(1024)S(1)} %convert_element_type.38, f32[512]{0:T(512)S(1)} %add_rsqrt_fusion), kind=kOutput, calls=%fused_computation.17 | convolution fusion | flops 3225419776 | bytes 11544576 | tf_op jit(solution)/shard_map/td,dhe->hte/dot_general | solution.py:95
  54.0 0.8 convolution_bitcast_fusion
  54.7 3.1 %add_bitcast_fusion = f32[4,512,384]{2,1,0:T(8,128)} fusion(f32[512,4,384]{2,0,1:T(8,128)S(1)} %fusion.6, f32[512,128,1]{1,0,2:T(8,128)S(1)} %convolution_bitcast_fusion, bf16[128,4,384]{0,2,1:T(8,128)(2,1)S(1)} %bitcast.138), kind=kOutput, calls=%fused_computation.15 | convolution fusion | flops 1208745984 | bytes 6946816 | tf_op jit(solution)/shard_map/tr,rhe->hte/dot_general | solution.py:98
  58.0 14.1 %reduce-scatter.3.cloned.1.call-done = f32[2,512,384]{2,1,0:T(8,128)} async-done(((f32[4,512,384]{2,1,0:T(8,128)}), f32[2,512,384]{2,1,0:T(8,128)}) %reduce-scatter.3.cloned.1.call-update) | async-done | bytes 1572880 | tf_op jit(solution)/shard_map/reduce_scatter | solution.py:104
  72.0 1.5 convert_element_type.40
  73.8 1.0 copy.27
  75.1 1.2 reduce-window.6
  76.7 4.9 %fusion = pred[512,8192]{1,0:T(8,128)(4,1)} fusion(s32[512]{0:T(512)S(1)} %iota_add_fusion, s32[8192]{0:T(1024)S(1)} %copy-done.4, s32[512]{0:T(512)S(1)} %dynamic_slice.51), kind=kLoop, calls=%fused_computation.5 | loop fusion | flops 12582912 | bytes 4231168 | tf_op jit(solution)/shard_map/and | solution.py:47
  81.6 65.8 %all-gather.5.cloned.1.call-done = bf16[8192,2,2,128]{3,0,1,2:T(8,128)(2,1)} async-done(((bf16[512,2,2,128]{3,0,1,2:T(8,128)(2,1)}), bf16[8192,2,2,128]{3,0,1,2:T(8,128)(2,1)}) %all-gather.5.cloned.1.call-update) | async-done | bytes 8388624 | tf_op jit(solution)/shard_map/all_gather | solution.py:118
  147.3 17.6 %select_reduce_fusion = (f32[2,512]{1,0:T(2,128)S(1)}, f32[2,512,8192]{2,1,0:T(8,128)}) fusion(pred[512,8192]{1,0:T(8,128)(4,1)} %fusion, bf16[8192,2,2,128]{3,0,1,2:T(8,128)(2,1)} %all-gather.5.cloned.1.call-done, bf16[2,512,3,128]{1,3,2,0:T(8,128)(2,1)S(1)} %bitcast.135), kind=kOutput, calls=%fused_computation.3 | convolution fusion | flops 2172648448 | bytes 42209280 | tf_op jit(solution)/shard_map/htd,shd->hts/dot_general | solution.py:52
  164.9 16.2 %convert_reduce_fusion = f32[2,512]{1,0:T(2,128)S(1)} fusion(f32[2,512]{1,0:T(2,128)S(1)} %broadcast_maximum_fusion, f32[2,512,8192]{2,1,0:T(8,128)} %get-tuple-element.19, pred[512,8192]{1,0:T(8,128)(4,1)} %fusion), kind=kLoop, calls=%fused_computation.1 | loop fusion | flops 50330624 | bytes 37756928 | tf_op jit(solution)/shard_map/reduce_sum | solution.py:60
  181.1 16.7 %fusion.12 = bf16[512,2,128]{0,2,1:T(8,128)(2,1)S(1)} fusion(bf16[8192,2,2,128]{3,0,1,2:T(8,128)(2,1)} %all-gather.5.cloned.1.call-done, f32[512,2]{0,1:T(2,128)S(1)} %bitcast.144, f32[2,512,8192]{2,1,0:T(8,128)} %get-tuple-element.19, f32[2,512]{1,0:T(2,128)S(1)} %broadcast_maximum_fusion, pred[512,8192]{1,0:T(8,128)(4,1)S(1)} %copy-done.1), kind=kOutput, calls=%fused_computation.24 | convolution fusion | flops 2181300224 | bytes 42213376 | tf_op jit(solution)/shard_map/hts,shd->htd/dot_general | solution.py:61
  197.9 2.1 convolution_convert_fusion
  200.1 0.7 fusion.9
  201.0 1.4 collective-permute-start
  202.4 2.9 %collective-permute-start.1 = (bf16[64,512]{1,0:T(8,128)(2,1)S(1)}, bf16[64,512]{1,0:T(8,128)(2,1)S(1)}, u32[]{:S(2)}, u32[]{:S(2)}) collective-permute-start(bf16[64,512]{1,0:T(8,128)(2,1)S(1)} %get-tuple-element.15), channel_id=1, source_target_pairs={{0,16},{8,24},{16,0},{24,8},{32,48},{40,56},{48,32},{56,40},{64,80... | collective-permute-start | bytes 196616 | tf_op jit(solution)/shard_map/ppermute | solution.py:34
  205.8 1.5 collective-permute-start.3
  207.3 3.7 %collective-permute-start.5 = (bf16[64,512]{1,0:T(8,128)(2,1)S(1)}, bf16[64,512]{1,0:T(8,128)(2,1)S(1)}, u32[]{:S(2)}, u32[]{:S(2)}) collective-permute-start(bf16[64,512]{1,0:T(8,128)(2,1)S(1)} %get-tuple-element.11), channel_id=1, source_target_pairs={{0,48},{8,56},{16,32},{24,40},{32,16},{40,24},{48,0},{56,8},{64,11... | collective-permute-start | bytes 196616 | tf_op jit(solution)/shard_map/ppermute | solution.py:34
  211.1 1.8 collective-permute-start.6
  213.0 3.1 %collective-permute-start.7 = (bf16[64,512]{1,0:T(8,128)(2,1)S(1)}, bf16[64,512]{1,0:T(8,128)(2,1)S(1)}, u32[]{:S(2)}, u32[]{:S(2)}) collective-permute-start(bf16[64,512]{1,0:T(8,128)(2,1)S(1)} %get-tuple-element.9), channel_id=1, source_target_pairs={{0,64},{8,72},{16,80},{24,88},{32,96},{40,104},{48,112},{56,120},{... | collective-permute-start | bytes 196616 | tf_op jit(solution)/shard_map/ppermute | solution.py:34
  216.2 5.1 %collective-permute-start.9 = (bf16[64,512]{1,0:T(8,128)(2,1)S(1)}, bf16[64,512]{1,0:T(8,128)(2,1)S(1)}, u32[]{:S(2)}, u32[]{:S(2)}) collective-permute-start(bf16[64,512]{1,0:T(8,128)(2,1)S(1)} %get-tuple-element.7), channel_id=1, source_target_pairs={{0,80},{8,88},{16,64},{24,72},{32,112},{40,120},{48,96},{56,104},{... | collective-permute-start | bytes 196616 | tf_op jit(solution)/shard_map/ppermute | solution.py:34
  221.2 2.1 collective-permute-start.10
  223.4 2.8 %collective-permute-start.11 = (bf16[64,512]{1,0:T(8,128)(2,1)S(1)}, bf16[64,512]{1,0:T(8,128)(2,1)S(1)}, u32[]{:S(2)}, u32[]{:S(2)}) collective-permute-start(bf16[64,512]{1,0:T(8,128)(2,1)S(1)} %get-tuple-element.5), channel_id=1, source_target_pairs={{0,96},{8,104},{16,112},{24,120},{32,64},{40,72},{48,80},{56,88},{... | collective-permute-start | bytes 196616 | tf_op jit(solution)/shard_map/ppermute | solution.py:34
  226.3 4.5 %collective-permute-start.13 = (bf16[64,512]{1,0:T(8,128)(2,1)S(1)}, bf16[64,512]{1,0:T(8,128)(2,1)S(1)}, u32[]{:S(2)}, u32[]{:S(2)}) collective-permute-start(bf16[64,512]{1,0:T(8,128)(2,1)S(1)} %get-tuple-element.3), channel_id=1, source_target_pairs={{0,112},{8,120},{16,96},{24,104},{32,80},{40,88},{48,64},{56,72},{... | collective-permute-start | bytes 196616 | tf_op jit(solution)/shard_map/ppermute | solution.py:34
  230.8 2.4 collective-permute-start.14
  233.3 1.0 collective-permute-done.13
  234.3 4.2 %collective-permute-done.14 = bf16[64,512]{1,0:T(8,128)(2,1)S(1)} collective-permute-done((bf16[64,512]{1,0:T(8,128)(2,1)S(1)}, bf16[64,512]{1,0:T(8,128)(2,1)S(1)}, u32[]{:S(2)}, u32[]{:S(2)}) %collective-permute-start.14) | collective-permute-done | bytes 65568 | tf_op jit(solution)/shard_map/ppermute | solution.py:34
  239.1 1.1 reshape_reshape.3
  (75 shorter events, 3.9 us)
Async XLA Ops:
  7.2 190.7 %copy-start = (bf16[256,2048]{1,0:T(8,128)(2,1)S(1)}, bf16[256,2048]{1,0:T(8,128)(2,1)}, u32[]{:S(2)}) copy-start(bf16[256,2048]{1,0:T(8,128)(2,1)} %param.13) | copy-start | bytes 3145732
  7.2 35.8 %all-gather.3.cloned.1.call-start = ((), (), s32[]{:S(2)}) async-start(), calls=%async_computation.2 | async-start | bytes 2621440 | tf_op jit(solution)/shard_map/all_gather | solution.py:77
  7.9 10.8 %copy-start.6 = (bf16[2048]{0:T(1024)(128)(2,1)S(1)}, bf16[2048]{0:T(1024)(128)(2,1)}, u32[]{:S(2)}) copy-start(bf16[2048]{0:T(1024)(128)(2,1)} %param.9) | copy-start | bytes 12292
  7.9 10.7 %copy-start.3 = (bf16[128,4,3,128]{3,1,2,0:T(4,128)(2,1)S(1)}, bf16[128,4,3,128]{3,1,2,0:T(4,128)(2,1)}, u32[]{:S(2)}) copy-start(bf16[128,4,3,128]{3,1,2,0:T(4,128)(2,1)} %param.12) | copy-start | bytes 1179652
  7.9 64.1 %reduce-scatter.3.cloned.1.call-start = ((), (), s32[]{:S(2)}) async-start(), calls=%async_computation.3 | async-start | bytes 4718592 | tf_op jit(solution)/shard_map/reduce_scatter | solution.py:104
  47.5 6.4 %copy-start.2 = (bf16[512,2048]{1,0:T(8,128)(2,1)S(1)}, bf16[512,2048]{1,0:T(8,128)(2,1)}, u32[]{:S(2)}) copy-start(bf16[512,2048]{1,0:T(8,128)(2,1)} %all-gather.3.cloned.1.call-done) | copy-start | bytes 6291460
  47.5 6.4 %copy-start.7 = (bf16[2048,128]{1,0:T(8,128)(2,1)S(1)}, bf16[2048,128]{1,0:T(8,128)(2,1)}, u32[]{:S(2)}) copy-start(bf16[2048,128]{1,0:T(8,128)(2,1)} %param.11) | copy-start | bytes 1572868
  57.9 17.2 %copy-start.5 = (s32[512,1]{0,1:T(1,128)S(1)}, s32[512,1]{0,1:T(1,128)}, u32[]{:S(2)}) copy-start(s32[512,1]{0,1:T(1,128)} %param.15) | copy-start | bytes 6148
  57.9 18.7 %copy-start.4 = (s32[8192]{0:T(1024)S(1)}, s32[8192]{0:T(1024)}, u32[]{:S(2)}) copy-start(s32[8192]{0:T(1024)} %param.14) | copy-start | bytes 98308
  57.9 89.4 %all-gather.5.cloned.1.call-start = ((), (), s32[]{:S(2)}) async-start(), calls=%async_computation.4 | async-start | bytes 8912896 | tf_op jit(solution)/shard_map/all_gather | solution.py:118
  74.9 165.3 %reduce-scatter.5.cloned.1.call-start = ((), (), s32[]{:S(2)}) async-start(), calls=%async_computation.5 | async-start | bytes 2359296 | tf_op jit(solution)/shard_map/reduce_scatter | solution.py:127
  164.9 16.2 %copy-start.1 = (pred[512,8192]{1,0:T(8,128)(4,1)S(1)}, pred[512,8192]{1,0:T(8,128)(4,1)}, u32[]{:S(2)}) copy-start(pred[512,8192]{1,0:T(8,128)(4,1)} %fusion) | copy-start | bytes 12582916
  201.0 6.3 %collective-permute-start = (bf16[64,512]{1,0:T(8,128)(2,1)S(1)}, bf16[64,512]{1,0:T(8,128)(2,1)S(1)}, u32[]{:S(2)}, u32[]{:S(2)}) collective-permute-start(bf16[64,512]{1,0:T(8,128)(2,1)S(1)} %get-tuple-element.16), channel_id=1, source_target_pairs={{0,8},{8,0},{16,24},{24,16},{32,40},{40,32},{48,56},{56,48},{64,72... | collective-permute-start | bytes 196616 | tf_op jit(solution)/shard_map/ppermute | solution.py:34
  202.4 8.7 %collective-permute-start.1 = (bf16[64,512]{1,0:T(8,128)(2,1)S(1)}, bf16[64,512]{1,0:T(8,128)(2,1)S(1)}, u32[]{:S(2)}, u32[]{:S(2)}) collective-permute-start(bf16[64,512]{1,0:T(8,128)(2,1)S(1)} %get-tuple-element.15), channel_id=1, source_target_pairs={{0,16},{8,24},{16,0},{24,8},{32,48},{40,56},{48,32},{56,40},{64,80... | collective-permute-start | bytes 196616 | tf_op jit(solution)/shard_map/ppermute | solution.py:34
  205.2 7.7 %collective-permute-start.2 = (bf16[64,512]{1,0:T(8,128)(2,1)S(1)}, bf16[64,512]{1,0:T(8,128)(2,1)S(1)}, u32[]{:S(2)}, u32[]{:S(2)}) collective-permute-start(bf16[64,512]{1,0:T(8,128)(2,1)S(1)} %get-tuple-element.14), channel_id=1, source_target_pairs={{0,24},{8,16},{16,8},{24,0},{32,56},{40,48},{48,40},{56,32},{64,88... | collective-permute-start | bytes 196616 | tf_op jit(solution)/shard_map/ppermute | solution.py:34
  205.8 10.2 %collective-permute-start.3 = (bf16[64,512]{1,0:T(8,128)(2,1)S(1)}, bf16[64,512]{1,0:T(8,128)(2,1)S(1)}, u32[]{:S(2)}, u32[]{:S(2)}) collective-permute-start(bf16[64,512]{1,0:T(8,128)(2,1)S(1)} %get-tuple-element.13), channel_id=1, source_target_pairs={{0,32},{8,40},{16,48},{24,56},{32,0},{40,8},{48,16},{56,24},{64,96... | collective-permute-start | bytes 196616 | tf_op jit(solution)/shard_map/ppermute | solution.py:34
  207.3 8.9 %collective-permute-start.4 = (bf16[64,512]{1,0:T(8,128)(2,1)S(1)}, bf16[64,512]{1,0:T(8,128)(2,1)S(1)}, u32[]{:S(2)}, u32[]{:S(2)}) collective-permute-start(bf16[64,512]{1,0:T(8,128)(2,1)S(1)} %get-tuple-element.12), channel_id=1, source_target_pairs={{0,40},{8,32},{16,56},{24,48},{32,8},{40,0},{48,24},{56,16},{64,10... | collective-permute-start | bytes 196616 | tf_op jit(solution)/shard_map/ppermute | solution.py:34
  207.3 13.9 %collective-permute-start.5 = (bf16[64,512]{1,0:T(8,128)(2,1)S(1)}, bf16[64,512]{1,0:T(8,128)(2,1)S(1)}, u32[]{:S(2)}, u32[]{:S(2)}) collective-permute-start(bf16[64,512]{1,0:T(8,128)(2,1)S(1)} %get-tuple-element.11), channel_id=1, source_target_pairs={{0,48},{8,56},{16,32},{24,40},{32,16},{40,24},{48,0},{56,8},{64,11... | collective-permute-start | bytes 196616 | tf_op jit(solution)/shard_map/ppermute | solution.py:34
  211.1 12.3 %collective-permute-start.6 = (bf16[64,512]{1,0:T(8,128)(2,1)S(1)}, bf16[64,512]{1,0:T(8,128)(2,1)S(1)}, u32[]{:S(2)}, u32[]{:S(2)}) collective-permute-start(bf16[64,512]{1,0:T(8,128)(2,1)S(1)} %get-tuple-element.10), channel_id=1, source_target_pairs={{0,56},{8,48},{16,40},{24,32},{32,24},{40,16},{48,8},{56,0},{64,12... | collective-permute-start | bytes 196616 | tf_op jit(solution)/shard_map/ppermute | solution.py:34
  213.0 13.2 %collective-permute-start.7 = (bf16[64,512]{1,0:T(8,128)(2,1)S(1)}, bf16[64,512]{1,0:T(8,128)(2,1)S(1)}, u32[]{:S(2)}, u32[]{:S(2)}) collective-permute-start(bf16[64,512]{1,0:T(8,128)(2,1)S(1)} %get-tuple-element.9), channel_id=1, source_target_pairs={{0,64},{8,72},{16,80},{24,88},{32,96},{40,104},{48,112},{56,120},{... | collective-permute-start | bytes 196616 | tf_op jit(solution)/shard_map/ppermute | solution.py:34
  216.0 10.3 %collective-permute-start.8 = (bf16[64,512]{1,0:T(8,128)(2,1)S(1)}, bf16[64,512]{1,0:T(8,128)(2,1)S(1)}, u32[]{:S(2)}, u32[]{:S(2)}) collective-permute-start(bf16[64,512]{1,0:T(8,128)(2,1)S(1)} %get-tuple-element.8), channel_id=1, source_target_pairs={{0,72},{8,64},{16,88},{24,80},{32,104},{40,96},{48,120},{56,112},{... | collective-permute-start | bytes 196616 | tf_op jit(solution)/shard_map/ppermute | solution.py:34
  216.2 14.6 %collective-permute-start.9 = (bf16[64,512]{1,0:T(8,128)(2,1)S(1)}, bf16[64,512]{1,0:T(8,128)(2,1)S(1)}, u32[]{:S(2)}, u32[]{:S(2)}) collective-permute-start(bf16[64,512]{1,0:T(8,128)(2,1)S(1)} %get-tuple-element.7), channel_id=1, source_target_pairs={{0,80},{8,88},{16,64},{24,72},{32,112},{40,120},{48,96},{56,104},{... | collective-permute-start | bytes 196616 | tf_op jit(solution)/shard_map/ppermute | solution.py:34
  221.2 12.0 %collective-permute-start.10 = (bf16[64,512]{1,0:T(8,128)(2,1)S(1)}, bf16[64,512]{1,0:T(8,128)(2,1)S(1)}, u32[]{:S(2)}, u32[]{:S(2)}) collective-permute-start(bf16[64,512]{1,0:T(8,128)(2,1)S(1)} %get-tuple-element.6), channel_id=1, source_target_pairs={{0,88},{8,80},{16,72},{24,64},{32,120},{40,112},{48,104},{56,96},{... | collective-permute-start | bytes 196616 | tf_op jit(solution)/shard_map/ppermute | solution.py:34
  223.4 9.9 %collective-permute-start.11 = (bf16[64,512]{1,0:T(8,128)(2,1)S(1)}, bf16[64,512]{1,0:T(8,128)(2,1)S(1)}, u32[]{:S(2)}, u32[]{:S(2)}) collective-permute-start(bf16[64,512]{1,0:T(8,128)(2,1)S(1)} %get-tuple-element.5), channel_id=1, source_target_pairs={{0,96},{8,104},{16,112},{24,120},{32,64},{40,72},{48,80},{56,88},{... | collective-permute-start | bytes 196616 | tf_op jit(solution)/shard_map/ppermute | solution.py:34
  226.2 7.1 %collective-permute-start.12 = (bf16[64,512]{1,0:T(8,128)(2,1)S(1)}, bf16[64,512]{1,0:T(8,128)(2,1)S(1)}, u32[]{:S(2)}, u32[]{:S(2)}) collective-permute-start(bf16[64,512]{1,0:T(8,128)(2,1)S(1)} %get-tuple-element.4), channel_id=1, source_target_pairs={{0,104},{8,96},{16,120},{24,112},{32,72},{40,64},{48,88},{56,80},{... | collective-permute-start | bytes 196616 | tf_op jit(solution)/shard_map/ppermute | solution.py:34
  226.3 8.0 %collective-permute-start.13 = (bf16[64,512]{1,0:T(8,128)(2,1)S(1)}, bf16[64,512]{1,0:T(8,128)(2,1)S(1)}, u32[]{:S(2)}, u32[]{:S(2)}) collective-permute-start(bf16[64,512]{1,0:T(8,128)(2,1)S(1)} %get-tuple-element.3), channel_id=1, source_target_pairs={{0,112},{8,120},{16,96},{24,104},{32,80},{40,88},{48,64},{56,72},{... | collective-permute-start | bytes 196616 | tf_op jit(solution)/shard_map/ppermute | solution.py:34
  230.8 7.7 %collective-permute-start.14 = (bf16[64,512]{1,0:T(8,128)(2,1)S(1)}, bf16[64,512]{1,0:T(8,128)(2,1)S(1)}, u32[]{:S(2)}, u32[]{:S(2)}) collective-permute-start(bf16[64,512]{1,0:T(8,128)(2,1)S(1)} %get-tuple-element.2), channel_id=1, source_target_pairs={{0,120},{8,112},{16,104},{24,96},{32,88},{40,80},{48,72},{56,64},{... | collective-permute-start | bytes 196616 | tf_op jit(solution)/shard_map/ppermute | solution.py:34
Sparse Core Ops, SparseCore 0:
  9.7 33.2 all-gather.2
  58.0 13.9 reduce-scatter.2
  75.0 72.3 all-gather.4
  200.1 34.0 reduce-scatter.4
